TPU v7x, 512 devices: a whole 4x8x8 slice. The times are simulated.
512 devices in a mesh: rep: 8 (over y_lo, core), seq: 2 (over y_hi), tp: 32 (over x, z).
Axes of the slice: x: 4, y: 8 (y_hi: 2, y_lo: 4; y = y_hi * 4 + y_lo), z: 8, core: 2. Of those that a mesh axis runs over, the one named last changes fastest.
Arguments:
- hidden: bfloat16 [3072, 8192], P('rep', ('seq', 'tp')), may hold values from -100 to 100
- gain: float32 [8192], replicated, may hold values from 0.1 to 1.9
- w_query: bfloat16 [8192, 8192], P('seq', 'tp'), may hold values from -1 to 1
- w_keyval: bfloat16 [2, 4096, 2048], P(None, 'tp'), may hold values from -1 to 1
- lengths: int32 [8, 2], replicated, may hold values from 128 to 192, as said below
- routes: int32 [8, 2], replicated, may hold values from 0 to 7, as said below
Outputs:
- attended: bfloat16 [3072, 8192], P(('rep', 'seq'), 'tp')
Inputs may be any that keep to these rules, and one draw needn't show every extreme that they name: `routes`: for each j, the responses j of the 8 rollout groups go to 8 different replicas, so each replica receives exactly 2 responses. `lengths`: the responses that one rollout group sends to one replica hold at most 192 tokens together, and in every draw some group sends exactly 192 tokens to one replica.
All inputs are finite; a program needn't handle non-finite values.
Results may differ from a plain program's by a relative error of at most 0.0076.
Values may be sent and summed in bfloat16 or wider, within the bound.
No kernel may reach another device: no remote copies, remote signals or barrier semaphores. Data moves between devices by JAX's collectives and lax.ppermute only.
A program may use at most 64 MiB of HBM per device.

v0:
```python
import math
import jax
import jax.numpy as jnp
from jax import lax
from jax.sharding import PartitionSpec as P

D = 8192
QH = 64
KVH = 8
HD = 128
RESP = 2
LMAX = 192
BUFFER = 384
ROPE_BASE = 500000.0
NORM_EPS = 1e-05
MASK_FILL = -1e30


def response_tables(lengths, routes):
    flat_len = lengths.reshape(-1)
    flat_route = routes.reshape(-1)
    response_ids = jnp.arange(flat_len.shape[0], dtype=jnp.int32)
    group_of = response_ids // RESP
    same_route = flat_route[:, None] == flat_route[None, :]
    same_group = group_of[:, None] == group_of[None, :]
    earlier = response_ids[None, :] < response_ids[:, None]
    dest_off = jnp.sum(jnp.where(same_route & earlier, flat_len[None, :], 0), axis=1)
    pair_off = jnp.sum(jnp.where(same_route & same_group & earlier, flat_len[None, :], 0), axis=1)
    src_start = jnp.sum(jnp.where(same_group & earlier, flat_len[None, :], 0), axis=1)
    return (flat_len, flat_route, group_of, dest_off, pair_off, src_start)


def locate(positions, replica, tables):
    flat_len, flat_route, group_of, dest_off, pair_off, src_start = tables
    response_ids = jnp.arange(flat_len.shape[0], dtype=jnp.int32)
    position_col = positions[:, None]
    inside = (
        (flat_route[None, :] == replica)
        & (dest_off[None, :] <= position_col)
        & (position_col < dest_off[None, :] + flat_len[None, :])
    )
    inside_int = inside.astype(jnp.int32)
    segment = jnp.sum(inside_int * (response_ids[None, :] + 1), axis=1) - 1
    seg_start = jnp.sum(inside_int * dest_off[None, :], axis=1)
    source_group = jnp.sum(inside_int * group_of[None, :], axis=1)
    pair_first = jnp.sum(inside_int * (dest_off - pair_off)[None, :], axis=1)
    source = jnp.sum(inside_int * src_start[None, :], axis=1)
    within = jnp.where(segment >= 0, positions - seg_start, 0)
    return (segment, within, source_group, pair_first, source)


def rotary(values_in, within):
    head_dim = values_in.shape[-1]
    half_dim = head_dim // 2
    freq_index = jnp.arange(half_dim, dtype=jnp.float32)
    inverse = jnp.power(ROPE_BASE, -2.0 * freq_index / head_dim)
    angles = within.astype(jnp.float32)[:, None] * inverse[None, :]
    cosine = jnp.cos(angles)[:, None, :]
    sine_part = jnp.sin(angles)[:, None, :]
    lower_half = values_in[..., :half_dim]
    upper_half = values_in[..., half_dim:]
    return jnp.concatenate(
        [
            lower_half * cosine - upper_half * sine_part,
            upper_half * cosine + lower_half * sine_part,
        ],
        axis=-1,
    )


def fill_rows(table, indices, present):
    taken = jnp.take(table, indices.reshape(-1), axis=0)
    return jnp.where(present.reshape(-1)[:, None], taken, jnp.zeros((), table.dtype))


def local(hidden, gain, w_query, w_keyval, lengths, routes):
    rep_count = lax.axis_size("rep")
    seq_count = lax.axis_size("seq")
    replica = lax.axis_index("rep")
    seq_index = lax.axis_index("seq")
    column = lax.axis_index("tp")
    feature_cols = hidden.shape[1]
    local_rows = BUFFER // seq_count
    capacity = (RESP + rep_count - 1) // rep_count * LMAX
    head_count = w_query.shape[1] // HD
    tables = response_tables(lengths, routes)
    flat_len, flat_route, group_of, dest_off, pair_off, src_start = tables
    my_len = lax.dynamic_slice_in_dim(flat_len, replica * RESP, RESP)
    my_route = lax.dynamic_slice_in_dim(flat_route, replica * RESP, RESP)
    my_pair = lax.dynamic_slice_in_dim(pair_off, replica * RESP, RESP)
    my_start = lax.dynamic_slice_in_dim(src_start, replica * RESP, RESP)
    slot_ids = jnp.arange(capacity, dtype=jnp.int32)
    targets = jnp.arange(rep_count, dtype=jnp.int32)
    block_off = jnp.broadcast_to(slot_ids[None, :], (rep_count, capacity))
    offsets = block_off[:, :, None]
    inside = (
        (my_route[None, None, :] == targets[:, None, None])
        & (my_pair[None, None, :] <= offsets)
        & (offsets < (my_pair + my_len)[None, None, :])
    )
    inside_int = inside.astype(jnp.int32)
    src_rows = jnp.sum(
        inside_int * (my_start[None, None, :] + offsets - my_pair[None, None, :]), axis=2
    )
    src_rows, present = (src_rows, jnp.any(inside, axis=2))
    outgoing = fill_rows(hidden, src_rows, present)
    incoming = lax.all_to_all(outgoing, "rep", split_axis=0, concat_axis=0, tiled=True)
    all_pos = jnp.arange(BUFFER, dtype=jnp.int32)
    segment, within, source_group, pair_first, source = locate(all_pos, replica, tables)
    gathered_idx = jnp.where(segment >= 0, source_group * capacity + all_pos - pair_first, 0)
    assembled = fill_rows(incoming, gathered_idx, segment >= 0)
    local_x = lax.all_to_all(
        assembled.reshape(BUFFER, 1, feature_cols), "seq", split_axis=0, concat_axis=1, tiled=True
    )
    query_pos = seq_index * local_rows + jnp.arange(local_rows, dtype=jnp.int32)
    query_info = locate(query_pos, replica, tables)
    query_seg = query_info[0]
    query_within = query_info[1]
    query_valid = query_seg >= 0
    gain_halves = gain.reshape(seq_count, D // seq_count)
    gain_local = lax.dynamic_slice_in_dim(gain_halves, column * feature_cols, feature_cols, 1)
    kv_head = column * head_count // (QH // KVH)
    query_weights = lax.all_gather(
        w_query.reshape(1, w_query.shape[0], w_query.shape[1]), "seq", axis=0, tiled=True
    )
    feature_piece = lax.all_gather(local_x, "tp", axis=2, tiled=True)
    scaled_piece = (feature_piece.astype(jnp.float32) * gain_halves[None]).astype(jnp.bfloat16)
    query_acc = jnp.einsum(
        "rsn,snf->rf", scaled_piece, query_weights, preferred_element_type=jnp.float32
    )
    squares = jnp.sum(jnp.square(feature_piece.astype(jnp.float32)), axis=(1, 2))
    inverse_rms = lax.rsqrt(squares / D + NORM_EPS)
    queries = rotary(
        inverse_rms[:, None, None] * query_acc.reshape(local_rows, head_count, HD), query_within
    ).astype(jnp.bfloat16)
    scaled_local = (local_x.astype(jnp.float32) * gain_local[None]).astype(jnp.bfloat16)
    kv_partial = jnp.einsum(
        "rsw,swc->rc", scaled_local, w_keyval, preferred_element_type=jnp.float32
    )
    kv_total = lax.psum(kv_partial, "tp")
    head_block = lax.dynamic_slice_in_dim(kv_total, kv_head * 2 * HD, 2 * HD, 1)
    keys = rotary(inverse_rms[:, None, None] * head_block[:, None, :HD], query_within)[:, 0].astype(
        jnp.bfloat16
    )
    values = (inverse_rms[:, None] * head_block[:, HD:]).astype(jnp.bfloat16)
    score_scale = 1.0 / math.sqrt(HD)
    running = jnp.full((local_rows, head_count), MASK_FILL, jnp.float32)
    key_part = lax.all_gather(keys, "seq", axis=0, tiled=True)
    value_part = lax.all_gather(values, "seq", axis=0, tiled=True)
    key_count = key_part.shape[0]
    key_pos = jnp.arange(key_count, dtype=jnp.int32)
    key_seg = locate(key_pos, replica, tables)[0]
    allowed = (key_seg[None, :] == query_seg[:, None]) & query_valid[:, None] & (
        key_pos[None, :] <= query_pos[:, None]
    ) | (key_pos[None, :] == query_pos[:, None])
    scores = (
        jnp.einsum("rhd,kd->rhk", queries, key_part, preferred_element_type=jnp.float32)
        * score_scale
    )
    scores = jnp.where(allowed[:, None, :], scores, MASK_FILL)
    new_max = jnp.maximum(running, jnp.max(scores, axis=2))
    prob_terms = jnp.where(allowed[:, None, :], jnp.exp(scores - new_max[:, :, None]), 0.0)
    totals = jnp.sum(prob_terms, axis=2)
    accum = jnp.einsum(
        "rhk,kd->rhd",
        prob_terms.astype(jnp.bfloat16),
        value_part,
        preferred_element_type=jnp.float32,
    )
    attended = (
        (accum / totals[:, :, None]).reshape(local_rows, head_count * HD).astype(jnp.bfloat16)
    )
    return jnp.where(query_valid[:, None], attended, jnp.zeros((), jnp.bfloat16))


def solution(mesh):
    in_specs = (P("rep", ("seq", "tp")), P(), P("seq", "tp"), P(None, "tp", None), P(), P())
    out_specs = P(("rep", "seq"), "tp")
    return jax.shard_map(local, mesh=mesh, in_specs=in_specs, out_specs=out_specs, check_vma=False)
```

profile of v0, /device:TPU:16, one launch (start us, length us, event | category | flops | bytes accessed | tf_op | source)
XLA Modules:
  0.0 440.9 jit_solution(4229495986316716021)
XLA Ops:
  6.5 0.8 copy.25
  7.5 0.8 copy.24
  8.4 0.2 select_reduce_fusion.7
  9.1 3.5 gather_fusion
  12.7 1.3 select_select_fusion
  14.0 9.1 %all-to-all-start = ((bf16[8,192,128]{2,1,0:T(8,128)(2,1)}), bf16[8,192,128]{2,1,0:T(8,128)(2,1)S(1)}, u32[]{:S(2)}, u32[]{:S(2)}) async-start(bf16[8,192,128]{2,1,0:T(8,128)(2,1)} %select_select_fusion), calls=%async_computation | async-start | bytes 786432 | tf_op jit(solution)/shard_map/all_to_all | solution.py:107
  23.1 0.1 select_reduce_fusion.1
  23.3 9.1 %all-to-all-done = bf16[8,192,128]{2,1,0:T(8,128)(2,1)S(1)} async-done(((bf16[8,192,128]{2,1,0:T(8,128)(2,1)}), bf16[8,192,128]{2,1,0:T(8,128)(2,1)S(1)}, u32[]{:S(2)}, u32[]{:S(2)}) %all-to-all-start) | async-done | bytes 393248 | tf_op jit(solution)/shard_map/all_to_all | solution.py:107
  32.4 1.4 gather_fusion.1
  33.8 0.2 fusion.37
  34.0 0.5 broadcast.494
  34.5 0.7 reduce.4
  35.2 10.6 %all_to_all.27 = bf16[2,2,12288]{2,1,0:T(2,128)(2,1)S(1)} all-to-all(bf16[2,2,12288]{2,1,0:T(2,128)(2,1)S(1)} %reshape.481), channel_id=1, replica_groups=mesh['rep'=8,'seq'=2,'tp'=32] {'seq'}, dimensions={0} | all-to-all | bytes 196608 | tf_op jit(solution)/shard_map/all_to_all | solution.py:112
  45.9 0.7 copy.29
  46.6 0.7 all-gather.8.cloned.1.call-update
  47.6 0.2 fusion.18
  47.8 2.5 convolution_bitcast_fusion
  50.3 0.4 multiply_cosine_fusion.1
  50.7 82.6 %all-gather.6.cloned.1.call-done = bf16[192,2,1,4096]{3,0,1,2:T(8,128)(2,1)} async-done(((bf16[192,2,1,128]{3,0,1,2:T(8,128)(2,1)}), bf16[192,2,1,4096]{3,0,1,2:T(8,128)(2,1)}) %all-gather.6.cloned.1.call-update) | async-done | bytes 3145744 | tf_op jit(solution)/shard_map/all_gather | solution.py:126
  133.3 2.6 fusion
  135.9 111.5 %all-gather.8.cloned.1.call-done = bf16[8192,256]{1,0:T(8,128)(2,1)} async-done(((bf16[4096,256]{1,0:T(8,128)(2,1)}), bf16[8192,256]{1,0:T(8,128)(2,1)}) %all-gather.8.cloned.1.call-update) | async-done | bytes 4194320 | tf_op jit(solution)/shard_map/all_gather | solution.py:123
  247.4 4.1 fusion.7
  251.7 161.3 %all-reduce.2.cloned.1.call-done = f32[192,2048]{1,0:T(8,128)} async-done(((f32[192,2048]{1,0:T(8,128)}), f32[192,2048]{1,0:T(8,128)}) %all-reduce.2.cloned.1.call-update) | async-done | bytes 1572880 | tf_op jit(solution)/shard_map/psum | solution.py:140
  412.9 1.0 fusion.30
  413.9 0.5 fusion.26
  414.5 9.2 %all-gather.2 = bf16[384,1,128]{2,0,1:T(8,128)(2,1)S(1)} all-gather(bf16[192,1,128]{2,0,1:T(8,128)(2,1)S(1)} %pad_maximum_fusion), channel_id=4, replica_groups=mesh['rep'=8,'seq'=2,'tp'=32] {'seq'}, dimensions={0}, use_global_device_ids=true | all-gather | bytes 147456 | tf_op jit(solution)/shard_map/all_gather | solution.py:148
  423.7 0.1 subtract_convert_fusion
  423.9 0.4 fusion.50
  424.3 8.7 %all_gather.15 = bf16[384,128]{1,0:T(8,128)(2,1)S(1)} all-gather(bf16[192,128]{1,0:T(8,128)(2,1)S(1)} %get-tuple-element.19), channel_id=1, replica_groups=mesh['rep'=8,'seq'=2,'tp'=32] {'seq'}, dimensions={0}, use_global_device_ids=true | all-gather | bytes 147456 | tf_op jit(solution)/shard_map/all_gather | solution.py:149
  433.0 0.3 fusion.12
  433.3 0.3 fusion.11
  433.7 0.7 bitcast_select_fusion
  (41 shorter events, 1.4 us)
Async XLA Ops:
  6.5 41.2 %copy-start = (bf16[2,128,2048]{2,1,0:T(8,128)(2,1)S(1)}, bf16[2,128,2048]{2,1,0:T(8,128)(2,1)}, u32[]{:S(2)}) copy-start(bf16[2,128,2048]{2,1,0:T(8,128)(2,1)} %param.9) | copy-start | bytes 3145732
  12.7 34.7 %copy-start.1 = (f32[8192]{0:T(1024)S(1)}, f32[8192]{0:T(1024)}, u32[]{:S(2)}) copy-start(f32[8192]{0:T(1024)} %param.7) | copy-start | bytes 98308
  14.0 18.4 %all-to-all-start = ((bf16[8,192,128]{2,1,0:T(8,128)(2,1)}), bf16[8,192,128]{2,1,0:T(8,128)(2,1)S(1)}, u32[]{:S(2)}, u32[]{:S(2)}) async-start(bf16[8,192,128]{2,1,0:T(8,128)(2,1)} %select_select_fusion), calls=%async_computation | async-start | bytes 786432 | tf_op jit(solution)/shard_map/all_to_all | solution.py:107
  23.1 110.2 %all-gather.6.cloned.1.call-start = ((), (), s32[]{:S(2)}) async-start(), calls=%async_computation.3 | async-start | bytes 3244032 | tf_op jit(solution)/shard_map/all_gather | solution.py:126
  46.6 200.9 %all-gather.8.cloned.1.call-start = ((), (), s32[]{:S(2)}) async-start(), calls=%async_computation.4 | async-start | bytes 6291456 | tf_op jit(solution)/shard_map/all_gather | solution.py:123
  47.3 365.6 %all-reduce.2.cloned.1.call-start = ((), (), s32[]{:S(2)}) async-start(), calls=%async_computation.2 | async-start | bytes 3145728 | tf_op jit(solution)/shard_map/psum | solution.py:140
Sparse Core Ops, SparseCore 0:
  46.7 86.6 all-gather.5
  135.4 111.9 all-gather.7
  250.8 162.0 all-reduce.1
where the time goes:
time: 441 us
  waiting for transfers between devices  365 us (83%)
  blocking collectives  28.5 us (6%)
  between operations  13.4 us (3%)
  starting transfers between devices  9.17 us (2%)
  other arithmetic  9.02 us (2%)
  local copies, waits for them, and re-layouts  8.3 us (2%)
  matrix products  7.34 us (2%)
    psum x1, waiting for transfers between devices, local(): kv_total = lax.psum(kv_partial, 'tp')  161 us
    all_gather x1, waiting for transfers between devices, local(): lax.all_gather(w_query.reshape(1, w_query.shape[0], w_query.shape[1]), 's...  111 us
    all_gather x1, waiting for transfers between devices, local(): feature_piece = lax.all_gather(local_x, 'tp', axis=2, tiled=True)  82.6 us
    all_to_all x1, blocking collectives, local(): lax.all_to_all(assembled.reshape(BUFFER, 1, feature_cols), 'seq', split_a...  10.6 us
    all_gather x1, blocking collectives, local(): key_part = lax.all_gather(keys, 'seq', axis=0, tiled=True)  9.25 us
    all_to_all x1, waiting for transfers between devices, local(): lax.all_to_all(outgoing, 'rep', split_axis=0, concat_axis=0, tiled=True)  9.09 us
    all_to_all x1, starting transfers between devices, local(): lax.all_to_all(outgoing, 'rep', split_axis=0, concat_axis=0, tiled=True)  9.08 us
  transfers between devices with their start and end apart: 4, of which 4 were waited for; matrix products, arithmetic and copies ran while one was open for 2% of the time, Pallas kernels for 0%

commit v1 on v0

--- a/solution.py
+++ b/solution.py
@@ -123,7 +123,9 @@
     query_weights = lax.all_gather(
         w_query.reshape(1, w_query.shape[0], w_query.shape[1]), "seq", axis=0, tiled=True
     )
-    feature_piece = lax.all_gather(local_x, "tp", axis=2, tiled=True)
+    ready = tuple((local_x for _ in range(lax.axis_size("tp"))))
+    r1 = jnp.concatenate(ready, axis=2)
+    feature_piece = lax.all_to_all(r1, axis_name="tp", split_axis=2, concat_axis=2, tiled=True)
     scaled_piece = (feature_piece.astype(jnp.float32) * gain_halves[None]).astype(jnp.bfloat16)
     query_acc = jnp.einsum(
         "rsn,snf->rf", scaled_piece, query_weights, preferred_element_type=jnp.float32

time: 441 us -> 313 us (0.71)
  waiting for transfers between devices: 365 us -> 181 us
  local copies, waits for them, and re-layouts: 8.3 us -> 50.9 us
  starting transfers between devices: 9.17 us -> 21.8 us
    all_gather x1, waiting for transfers between devices: 111 us -> 0.02 us  [local(): lax.all_gather(w_query.reshape(1, w_query.shape[0], w_query.shape[1]), 's...]
    all_to_all x0 -> x1, waiting for transfers between devices: none -> 103 us  [local(): lax.all_to_all(r1, axis_name='tp', split_axis=2, concat_axis=2, tiled=True)]
    psum x1, waiting for transfers between devices: 161 us -> 67.9 us  [local(): kv_total = lax.psum(kv_partial, 'tp')]
    all_gather x1 -> x0, waiting for transfers between devices: 82.6 us -> none  [local(): feature_piece = lax.all_gather(local_x, 'tp', axis=2, tiled=True)]
    unnamed x9 -> x40, local copies, waits for them, and re-layouts: 2.38 us -> 22.4 us
    all_to_all x0 -> x1, starting transfers between devices: none -> 12.6 us  [local(): lax.all_to_all(r1, axis_name='tp', split_axis=2, concat_axis=2, tiled=True)]
    concatenate x0 -> x2, local copies, waits for them, and re-layouts: none -> 11.6 us  [local(): r1 = jnp.concatenate(ready, axis=2)]
    all_to_all x0 -> x1, local copies, waits for them, and re-layouts: none -> 11 us  [local(): lax.all_to_all(r1, axis_name='tp', split_axis=2, concat_axis=2, tiled=True)]
  transfers between devices with their start and end apart: 4 -> 4, of which waited for: 4 -> 3; matrix products, arithmetic and copies ran while one was open for 2% -> 6% of each run, Pallas kernels for 0% -> 0%
where the time goes in v1:
time: 313 us; the launch traced here: 312 us
  waiting for transfers between devices  181 us (58%)
  local copies, waits for them, and re-layouts  50.9 us (16%)
  blocking collectives  28.6 us (9%)
  starting transfers between devices  21.8 us (7%)
  between operations  15.1 us (5%)
  other arithmetic  9.02 us (3%)
  matrix products  6.42 us (2%)
    all_to_all x1, waiting for transfers between devices, local(): lax.all_to_all(r1, axis_name='tp', split_axis=2, concat_axis=2, tiled=True)  103 us
    psum x1, waiting for transfers between devices, local(): kv_total = lax.psum(kv_partial, 'tp')  67.9 us
    unnamed x40, local copies, waits for them, and re-layouts  22.4 us
    all_to_all x1, starting transfers between devices, local(): lax.all_to_all(r1, axis_name='tp', split_axis=2, concat_axis=2, tiled=True)  12.6 us
    concatenate x2, local copies, waits for them, and re-layouts, local(): r1 = jnp.concatenate(ready, axis=2)  11.6 us
    all_to_all x1, local copies, waits for them, and re-layouts, local(): lax.all_to_all(r1, axis_name='tp', split_axis=2, concat_axis=2, tiled=True)  11 us
    all_to_all x1, blocking collectives, local(): lax.all_to_all(assembled.reshape(BUFFER, 1, feature_cols), 'seq', split_a...  10.6 us
    all_gather x1, blocking collectives, local(): key_part = lax.all_gather(keys, 'seq', axis=0, tiled=True)  9.25 us
  transfers between devices with their start and end apart: 4, of which 3 were waited for; matrix products, arithmetic and copies ran while one was open for 6% of the time, Pallas kernels for 0%

profile of v1, /device:TPU:16, one launch (start us, length us, event | category | flops | bytes accessed | tf_op | source)
XLA Modules:
  0.0 312.5 jit_solution(17121237374833972818)
XLA Ops:
  7.4 0.8 copy.39
  8.3 0.8 copy.38
  10.0 3.5 %gather_fusion = bf16[1536,128]{1,0:T(8,128)(2,1)S(1)} fusion(bf16[384,128]{1,0:T(8,128)(2,1)} %param.6, s32[2048]{0:T(1024)S(1)} %pad_clamp_fusion), kind=kCustom, calls=%fused_computation | custom fusion | bytes 792576 | tf_op jit(solution)/shard_map/jit(_take)/gather | solution.py:72
  13.5 1.3 select_select_fusion
  14.8 9.1 %all-to-all-start = ((bf16[8,192,128]{2,1,0:T(8,128)(2,1)}), bf16[8,192,128]{2,1,0:T(8,128)(2,1)S(1)}, u32[]{:S(2)}, u32[]{:S(2)}) async-start(bf16[8,192,128]{2,1,0:T(8,128)(2,1)} %select_select_fusion), calls=%async_computation | async-start | bytes 786432 | tf_op jit(solution)/shard_map/all_to_all | solution.py:107
  24.1 9.1 %all-to-all-done = bf16[8,192,128]{2,1,0:T(8,128)(2,1)S(1)} async-done(((bf16[8,192,128]{2,1,0:T(8,128)(2,1)}), bf16[8,192,128]{2,1,0:T(8,128)(2,1)S(1)}, u32[]{:S(2)}, u32[]{:S(2)}) %all-to-all-start) | async-done | bytes 393248 | tf_op jit(solution)/shard_map/all_to_all | solution.py:107
  33.2 1.4 gather_fusion.1
  36.0 10.6 %all_to_all.32 = bf16[2,2,12288]{2,1,0:T(2,128)(2,1)S(1)} all-to-all(bf16[2,2,12288]{2,1,0:T(2,128)(2,1)S(1)} %reshape.478), channel_id=1, replica_groups=mesh['rep'=8,'seq'=2,'tp'=32] {'seq'}, dimensions={0} | all-to-all | bytes 196608 | tf_op jit(solution)/shard_map/all_to_all | solution.py:112
  47.4 0.7 constant_dynamic-update-slice_fusion.30
  48.1 0.7 constant_dynamic-update-slice_fusion.29
  50.1 0.7 constant_dynamic-update-slice_fusion.26
  51.4 0.7 constant_dynamic-update-slice_fusion.24
  52.7 0.7 constant_dynamic-update-slice_fusion.22
  54.1 0.7 constant_dynamic-update-slice_fusion.20
  58.7 0.7 constant_dynamic-update-slice_fusion.13
  59.4 0.7 constant_dynamic-update-slice_fusion.12
  61.4 0.7 constant_dynamic-update-slice_fusion.9
  65.4 0.7 constant_dynamic-update-slice_fusion.3
  67.4 0.7 constant_dynamic-update-slice_fusion
  68.1 11.0 %copy.41 = bf16[192,2,4096]{0,1,2:T(2,128)(2,1)} copy(bf16[192,2,4096]{2,0,1:T(8,128)(2,1)} %constant_dynamic-update-slice_fusion) | data formatting | bytes 6291456 | tf_op jit(solution)/shard_map/concatenate | solution.py:127
  79.0 12.6 %all-to-all-start.2 = ((bf16[192,2,4096]{0,1,2:T(2,128)(2,1)}), bf16[192,2,4096]{0,1,2:T(2,128)(2,1)}, u32[]{:S(2)}, u32[]{:S(2)}) async-start(bf16[192,2,4096]{0,1,2:T(2,128)(2,1)} %copy.41), calls=%async_computation.2 | async-start | bytes 8388608 | tf_op jit(solution)/shard_map/all_to_all | solution.py:128
  91.7 0.7 all-gather.4.cloned.1.call-update
  92.8 1.5 convolution_bitcast_fusion
  94.8 102.9 %all-to-all-done.2 = bf16[192,2,4096]{0,1,2:T(2,128)(2,1)} async-done(((bf16[192,2,4096]{0,1,2:T(2,128)(2,1)}), bf16[192,2,4096]{0,1,2:T(2,128)(2,1)}, u32[]{:S(2)}, u32[]{:S(2)}) %all-to-all-start.2) | async-done | bytes 3145760 | tf_op jit(solution)/shard_map/all_to_all | solution.py:128
  197.7 11.0 %copy.42 = bf16[192,2,4096]{2,0,1:T(8,128)(2,1)} copy(bf16[192,2,4096]{0,1,2:T(2,128)(2,1)} %all-to-all-done.2) | data formatting | bytes 6291456 | tf_op jit(solution)/shard_map/all_to_all | solution.py:128
  208.7 2.6 fusion
  211.3 4.2 %fusion.6 = f32[24,2,8,128]{3,2,1,0:T(8,128)S(1)} fusion(bf16[2,4096,256]{2,1,0:T(8,128)(2,1)} %bitcast.71, bf16[192,2,4096]{2,0,1:T(8,128)(2,1)} %copy.42, f32[2,4096]{1,0:T(2,128)S(1)} %mul.228), kind=kOutput, calls=%fused_computation.12 | convolution fusion | flops 810024960 | bytes 7569408 | tf_op jit(solution)/shard_map/rsn,snf->rf/dot_general | solution.py:130
  215.6 67.9 %all-reduce.2.cloned.1.call-done = f32[192,2048]{1,0:T(8,128)} async-done(((f32[192,2048]{1,0:T(8,128)}), f32[192,2048]{1,0:T(8,128)}) %all-reduce.2.cloned.1.call-update) | async-done | bytes 1572880 | tf_op jit(solution)/shard_map/psum | solution.py:142
  283.5 1.0 fusion.27
  285.1 9.2 %all-gather.1 = bf16[384,1,128]{2,0,1:T(8,128)(2,1)S(1)} all-gather(bf16[192,1,128]{2,0,1:T(8,128)(2,1)S(1)} %pad_maximum_fusion), channel_id=3, replica_groups=mesh['rep'=8,'seq'=2,'tp'=32] {'seq'}, dimensions={0}, use_global_device_ids=true | all-gather | bytes 147456 | tf_op jit(solution)/shard_map/all_gather | solution.py:150
  294.9 8.8 %all_gather.11 = bf16[384,128]{1,0:T(8,128)(2,1)S(1)} all-gather(bf16[192,128]{1,0:T(8,128)(2,1)S(1)} %get-tuple-element.19), channel_id=1, replica_groups=mesh['rep'=8,'seq'=2,'tp'=32] {'seq'}, dimensions={0}, use_global_device_ids=true | all-gather | bytes 147456 | tf_op jit(solution)/shard_map/all_gather | solution.py:151
  304.3 0.7 bitcast_select_fusion
  (74 shorter events, 19.2 us)
Async XLA Ops:
  7.4 85.5 %copy-start = (bf16[2,128,2048]{2,1,0:T(8,128)(2,1)S(1)}, bf16[2,128,2048]{2,1,0:T(8,128)(2,1)}, u32[]{:S(2)}) copy-start(bf16[2,128,2048]{2,1,0:T(8,128)(2,1)} %param.9) | copy-start | bytes 3145732
  14.8 18.4 %all-to-all-start = ((bf16[8,192,128]{2,1,0:T(8,128)(2,1)}), bf16[8,192,128]{2,1,0:T(8,128)(2,1)S(1)}, u32[]{:S(2)}, u32[]{:S(2)}) async-start(bf16[8,192,128]{2,1,0:T(8,128)(2,1)} %select_select_fusion), calls=%async_computation | async-start | bytes 786432 | tf_op jit(solution)/shard_map/all_to_all | solution.py:107
  79.0 13.4 %copy-start.1 = (f32[8192]{0:T(1024)S(1)}, f32[8192]{0:T(1024)}, u32[]{:S(2)}) copy-start(f32[8192]{0:T(1024)} %param.7) | copy-start | bytes 98308
  79.0 118.7 %all-to-all-start.2 = ((bf16[192,2,4096]{0,1,2:T(2,128)(2,1)}), bf16[192,2,4096]{0,1,2:T(2,128)(2,1)}, u32[]{:S(2)}, u32[]{:S(2)}) async-start(bf16[192,2,4096]{0,1,2:T(2,128)(2,1)} %copy.41), calls=%async_computation.2 | async-start | bytes 8388608 | tf_op jit(solution)/shard_map/all_to_all | solution.py:128
  91.6 119.7 %all-gather.4.cloned.1.call-start = ((), (), s32[]{:S(2)}) async-start(), calls=%async_computation.4 | async-start | bytes 6291456 | tf_op jit(solution)/shard_map/all_gather | solution.py:123
  92.4 191.1 %all-reduce.2.cloned.1.call-start = ((), (), s32[]{:S(2)}) async-start(), calls=%async_computation.3 | async-start | bytes 3145728 | tf_op jit(solution)/shard_map/psum | solution.py:142
Sparse Core Ops, SparseCore 0:
  94.8 111.0 all-gather.3
Sparse Core Ops, SparseCore 1:
  96.2 187.2 all-reduce.1
